TPU v7x, 512 devices: a whole 4x8x8 slice. The times are simulated.
512 devices in a mesh: dp: 64 (over z, x, core), mp: 8 (over y).
Axes of the slice: x: 4, y: 8, z: 8, core: 2. Of those that a mesh axis runs over, the one named last changes fastest.
Arguments:
- micro_grads: bfloat16 [64, 2, 768, 768], P('dp', None, None, 'mp'), may hold values from -16 to 16
- master: float32 [768, 768], P('dp', 'mp'), may hold values from -0.21875 to 0.21875
- moment: float32 [768, 768], P('dp', 'mp'), may hold values from -1.5 to 1.5
- second: float32 [768, 768], P('dp', 'mp'), may hold values from 0.001 to 0.1
- left_basis: float32 [768, 768], P(None, 'dp'), may hold values from -0.21875 to 0.21875
- right_basis: float32 [768, 768], P(None, 'mp'), may hold values from -0.21875 to 0.21875
- left_stat: float32 [768, 768], P('mp'), may hold values from -2 to 5, as said below
- right_stat: float32 [768, 768], P('mp'), may hold values from -2 to 5, as said below
Outputs:
- weights_block: bfloat16 [768, 768], P(None, 'mp')
- new_master: float32 [768, 768], P('dp', 'mp')
- new_moment: float32 [768, 768], P('dp', 'mp')
- new_second: float32 [768, 768], P('dp', 'mp')
- new_left_stat: float32 [768, 768], P('mp')
- new_right_stat: float32 [768, 768], P('mp')
- new_left_basis: float32 [768, 768], P('mp')
- new_right_basis: float32 [768, 768], P('mp')
Inputs may be any that keep to these rules, and one draw needn't show every extreme that they name: `left_stat`: symmetric. `right_stat`: symmetric.
All inputs are finite; a program needn't handle non-finite values.
Results may differ from a plain program's by a relative error of at most 0.004.
The roundings to bfloat16 on the way count: a program that leaves them out, or rounds other values in their place, can miss the bound.
Values may be sent and summed in bfloat16 or wider, within the bound.
No kernel may reach another device: no remote copies, remote signals or barrier semaphores. Data moves between devices by JAX's collectives and lax.ppermute only.
A program may use at most 64 MiB of HBM per device.

v0:
```python
import jax
import jax.numpy as jnp
from jax import lax
from jax.sharding import PartitionSpec as P

beta_one = 0.9
beta_two = 0.95
beta_stat = 0.95
learn_rate = 0.02
adam_eps = 1e-08
norm_eps = 1e-06
quint_a = 1.875
quint_b = -1.25
quint_c = 0.375
highest = lax.Precision.HIGHEST


def for_sending(x):

    def short(part):
        return part.astype(jnp.bfloat16) if part.dtype == jnp.float32 else part

    return jax.tree.map(short, x)


def all_rows(pair):
    return jax.tree.map(
        lambda part, own: part.astype(own.dtype),
        lax.all_gather(for_sending(pair), "mp", axis=0, tiled=True),
        pair,
    )


def row_gram(row_part, whole_part):
    return lax.dot_general(
        row_part, whole_part, (((1,), (1,)), ((), ())), preferred_element_type=jnp.float32
    )


def per_device(micro_grads, master, moment, second, left_basis, right_basis, left_stat, right_stat):
    dp_count = lax.axis_size("dp")
    micro_count = micro_grads.shape[1]
    local_sum = jnp.sum(micro_grads[0], axis=0, dtype=jnp.float32)
    grad_piece = lax.psum_scatter(local_sum, "dp", scatter_dimension=0, tiled=True) / (
        micro_count * dp_count
    )
    new_moment = beta_one * moment + (1.0 - beta_one) * grad_piece
    grad_cols, moment_cols, left_full = (
        lax.all_gather(grad_piece, "dp", axis=0, tiled=True),
        lax.all_gather(new_moment, "dp", axis=0, tiled=True),
        lax.all_gather(left_basis, "dp", axis=1, tiled=True),
    )
    grad_full, moment_full, right_full = (
        lax.all_gather(grad_cols, "mp", axis=1, tiled=True),
        lax.all_gather(moment_cols, "mp", axis=1, tiled=True),
        lax.all_gather(right_basis, "mp", axis=1, tiled=True),
    )

    def rotate(matrix):
        left_part = lax.dot_general(left_basis, matrix, (((0,), (0,)), ((), ())), precision=highest)
        return jnp.dot(left_part, right_basis, precision=highest)

    rot_grad = rotate(grad_full)
    rot_moment = rotate(moment_full)
    new_second = beta_two * second + (1.0 - beta_two) * rot_grad * rot_grad
    rot_step = rot_moment / (jnp.sqrt(new_second) + adam_eps)
    basis_rows = right_basis
    back_half = lax.psum_scatter(
        lax.dot_general(basis_rows, rot_step, (((1,), (1,)), ((), ())), precision=highest),
        "mp",
        scatter_dimension=0,
        tiled=True,
    )
    basis_rows = left_basis
    step_piece = lax.psum_scatter(
        lax.dot_general(basis_rows, back_half, (((1,), (1,)), ((), ())), precision=highest),
        "dp",
        scatter_dimension=0,
        tiled=True,
    )
    new_master = master - learn_rate * step_piece
    weights_block = lax.all_gather(new_master.astype(jnp.bfloat16), "dp", axis=0, tiled=True)
    band_width = right_basis.shape[1]
    band_start = lax.axis_index("mp") * band_width
    grad_band = lax.dynamic_slice_in_dim(grad_full, band_start, band_width, 0)
    grad_strip = lax.dynamic_slice_in_dim(grad_full, band_start, band_width, 1)
    left_outer = lax.dot_general(grad_band, grad_full, (((1,), (1,)), ((), ())), precision=highest)
    right_outer = lax.dot_general(
        grad_strip, grad_full, (((0,), (0,)), ((), ())), precision=highest
    )
    new_left_stat = beta_stat * left_stat + (1.0 - beta_stat) * left_outer
    new_right_stat = beta_stat * right_stat + (1.0 - beta_stat) * right_outer
    order_count = left_stat.shape[1]
    power_left = jnp.dot(
        new_left_stat.astype(jnp.bfloat16),
        left_full.astype(jnp.bfloat16),
        preferred_element_type=jnp.float32,
    )
    power_right = jnp.dot(
        new_right_stat.astype(jnp.bfloat16),
        right_full.astype(jnp.bfloat16),
        preferred_element_type=jnp.float32,
    )
    total_left, total_right = lax.psum(
        (jnp.sum(power_left * power_left), jnp.sum(power_right * power_right)), "mp"
    )
    start_left = lax.optimization_barrier(
        (power_left * lax.rsqrt(total_left * (4.0 / order_count) + norm_eps)).astype(jnp.bfloat16)
    )
    start_right = lax.optimization_barrier(
        (power_right * lax.rsqrt(total_right * (4.0 / order_count) + norm_eps)).astype(jnp.bfloat16)
    )
    start_rows = (start_left, start_right)
    start_whole = all_rows(start_rows)
    gram_rows = tuple(
        (
            lax.optimization_barrier(row_gram(row_part, whole_part).astype(jnp.bfloat16))
            for row_part, whole_part in zip(start_rows, start_whole)
        )
    )
    gram_whole = all_rows(gram_rows)
    middle_rows = []
    for row_part, gram_part, gram_all, whole_part in zip(
        start_rows, gram_rows, gram_whole, start_whole
    ):
        square = jnp.dot(gram_part, gram_all, preferred_element_type=jnp.float32)
        poly_rows = (quint_b * gram_part.astype(jnp.float32) + quint_c * square).astype(
            jnp.bfloat16
        )
        middle = quint_a * row_part.astype(jnp.float32) + jnp.dot(
            poly_rows, whole_part, preferred_element_type=jnp.float32
        )
        middle_rows.append(lax.optimization_barrier(middle.astype(jnp.bfloat16)))
    middle_whole = all_rows(tuple(middle_rows))
    new_bases = []
    for row_part, whole_part in zip(middle_rows, middle_whole):
        gram_two = row_gram(row_part, whole_part).astype(jnp.bfloat16)
        new_bases.append(
            1.5 * row_part.astype(jnp.float32)
            - 0.5 * jnp.dot(gram_two, whole_part, preferred_element_type=jnp.float32)
        )
    return (
        weights_block,
        new_master,
        new_moment,
        new_second,
        new_left_stat,
        new_right_stat,
        new_bases[0],
        new_bases[1],
    )


def solution(mesh):
    in_specs = (
        P("dp", None, None, "mp"),
        P("dp", "mp"),
        P("dp", "mp"),
        P("dp", "mp"),
        P(None, "dp"),
        P(None, "mp"),
        P("mp", None),
        P("mp", None),
    )
    out_specs = (
        P(None, "mp"),
        P("dp", "mp"),
        P("dp", "mp"),
        P("dp", "mp"),
        P("mp", None),
        P("mp", None),
        P("mp", None),
        P("mp", None),
    )
    return jax.shard_map(
        per_device, mesh=mesh, in_specs=in_specs, out_specs=out_specs, check_vma=False
    )
```

profile of v0, /device:TPU:2, one launch (start us, length us, event | category | flops | bytes accessed | tf_op | source)
XLA Modules:
  0.0 924.6 jit_solution(14783238774417573509)
XLA Ops:
  12.0 195.7 %all-reduce.6.cloned.1.call-done = f32[768,96]{1,0:T(8,128)} async-done(((f32[768,96]{1,0:T(8,128)}), f32[768,96]{1,0:T(8,128)}) %all-reduce.6.cloned.1.call-update) | async-done | bytes 294928
  208.4 48.3 %all-gather.1 = f32[64,12,96]{2,1,0:T(8,128)S(1)} all-gather(f32[1,12,96]{2,1,0:T(8,128)S(1)} %get-tuple-element.36), channel_id=1, replica_groups=mesh['dp'=64,'mp'=8] {'dp'}, dimensions={0}, use_global_device_ids=true | all-gather | bytes 299520 | tf_op jit(solution)/shard_map/all_gather | solution.py:49
  258.4 48.9 %all-gather = f32[64,12,96]{2,1,0:T(8,128)S(1)} all-gather(f32[1,12,96]{2,1,0:T(8,128)S(1)} %bitcast.49), channel_id=1, replica_groups=mesh['dp'=64,'mp'=8] {'dp'}, dimensions={0}, use_global_device_ids=true | all-gather | bytes 299520 | tf_op jit(solution)/shard_map/all_gather | solution.py:50
  308.3 3.2 reshape.25
  311.5 26.6 %all-gather.17.cloned.1.call-done = f32[768,768]{0,1:T(8,128)} async-done(((f32[768,96]{0,1:T(8,128)}), f32[768,768]{0,1:T(8,128)}) %all-gather.17.cloned.1.call-update) | async-done | bytes 2359312 | tf_op jit(solution)/shard_map/all_gather | solution.py:54
  338.2 3.7 fusion.3
  341.9 3.2 multiply_reduce_fusion.1
  347.5 33.6 %all-gather.25.cloned.1.call-done = bf16[768,768]{0,1:T(8,128)(2,1)} async-done(((bf16[768,96]{0,1:T(8,128)(2,1)}), bf16[768,768]{0,1:T(8,128)(2,1)}) %all-gather.25.cloned.1.call-update) | async-done | bytes 1179664 | tf_op jit(solution)/shard_map/all_gather | solution.py:56
  383.5 16.6 %all-reduce.2 = (f32[]{:T(128)}, f32[]{:T(128)}) all-reduce(f32[]{:T(128)} %get-tuple-element.38, f32[]{:T(128)} %get-tuple-element.40), channel_id=1, replica_groups=mesh['dp'=64,'mp'=8] {'mp'}, use_global_device_ids=true, to_apply=%region_5.0 | all-reduce | flops 2 | bytes 16 | tf_op jit(solution)/shard_map/psum | solution.py:104
  403.2 2.8 fusion.35
  406.4 20.7 %all-gather.15.cloned.1.call-done = f32[768,768]{0,1:T(8,128)} async-done(((f32[768,96]{0,1:T(8,128)}), f32[768,768]{0,1:T(8,128)}) %all-gather.15.cloned.1.call-update) | async-done | bytes 2359312 | tf_op jit(solution)/shard_map/all_gather | solution.py:55
  427.1 3.7 fusion.34
  432.5 37.3 %all-gather.19.cloned.1.call-done = bf16[768,768]{1,0:T(8,128)(2,1)} async-done(((bf16[96,768]{1,0:T(8,128)(2,1)}), bf16[768,768]{1,0:T(8,128)(2,1)}) %all-gather.19.cloned.1.call-update) | async-done | bytes 1179664 | tf_op jit(solution)/shard_map/all_gather | solution.py:29
  472.4 40.6 %all-gather.27.cloned.1.call-done = bf16[768,768]{1,0:T(8,128)(2,1)} async-done(((bf16[96,768]{1,0:T(8,128)(2,1)}), bf16[768,768]{1,0:T(8,128)(2,1)}) %all-gather.27.cloned.1.call-update) | async-done | bytes 1179664 | tf_op jit(solution)/shard_map/all_gather | solution.py:29
  515.4 38.7 %reduce-scatter.5.cloned.1.call-done = f32[96,12]{1,0:T(8,128)} async-done(((f32[768,12]{1,0:T(8,128)}), f32[96,12]{1,0:T(8,128)}) %reduce-scatter.5.cloned.1.call-update) | async-done | bytes 4624
  556.1 41.1 %all-gather.21.cloned.1.call-done = bf16[768,768]{1,0:T(8,128)(2,1)} async-done(((bf16[96,768]{1,0:T(8,128)(2,1)}), bf16[768,768]{1,0:T(8,128)(2,1)}) %all-gather.21.cloned.1.call-update) | async-done | bytes 1179664 | tf_op jit(solution)/shard_map/all_gather | solution.py:29
  597.3 2.5 fusion.9
  599.9 39.5 %all-gather.29.cloned.1.call-done = bf16[768,768]{1,0:T(8,128)(2,1)} async-done(((bf16[96,768]{1,0:T(8,128)(2,1)}), bf16[768,768]{1,0:T(8,128)(2,1)}) %all-gather.29.cloned.1.call-update) | async-done | bytes 1179664 | tf_op jit(solution)/shard_map/all_gather | solution.py:29
  639.4 2.5 fusion.11
  642.1 187.5 %all-reduce.8.cloned.1.call-done = f32[768,96]{0,1:T(8,128)} async-done(((f32[768,96]{0,1:T(8,128)}), f32[768,96]{0,1:T(8,128)}) %all-reduce.8.cloned.1.call-update) | async-done | bytes 294928
  830.7 41.5 %all-gather.2 = bf16[64,12,96]{2,1,0:T(8,128)(2,1)S(1)} all-gather(bf16[1,12,96]{2,1,0:T(8,128)(2,1)S(1)} %copy.26), channel_id=1, replica_groups=mesh['dp'=64,'mp'=8] {'dp'}, dimensions={0}, use_global_device_ids=true | all-gather | bytes 149760 | tf_op jit(solution)/shard_map/all_gather | solution.py:82
  873.7 3.1 fusion.6
  876.9 38.0 %all-gather.31.cloned.1.call-done = bf16[768,768]{1,0:T(8,128)(2,1)} async-done(((bf16[96,768]{1,0:T(8,128)(2,1)}), bf16[768,768]{1,0:T(8,128)(2,1)}) %all-gather.31.cloned.1.call-update) | async-done | bytes 1179664 | tf_op jit(solution)/shard_map/all_gather | solution.py:29
  914.9 3.1 fusion.4
  (99 shorter events, 25.8 us)
Async XLA Ops:
  7.2 200.5 %copy-start.21 = (f32[12,96]{1,0:T(8,128)S(1)}, f32[12,96]{1,0:T(8,128)}, u32[]{:S(2)}) copy-start(f32[12,96]{1,0:T(8,128)} %param.10) | copy-start | bytes 13828
  7.2 200.4 %all-reduce.6.cloned.1.call-start = ((), (), s32[]{:S(2)}) async-start(), calls=%async_computation.12 | async-start | bytes 786432
  9.2 299.1 %all-gather.33.cloned.1.call-start = ((), (), s32[]{:S(2)}) async-start(), calls=%async_computation.10 | async-start | bytes 1597440 | tf_op jit(solution)/shard_map/all_gather | solution.py:51
  10.0 328.2 %all-gather.17.cloned.1.call-start = ((), (), s32[]{:S(2)}) async-start(), calls=%async_computation.2 | async-start | bytes 2654208 | tf_op jit(solution)/shard_map/all_gather | solution.py:54
  208.3 50.0 %copy-start.17 = (f32[12,96]{1,0:T(8,128)}, f32[12,96]{1,0:T(8,128)S(1)}, u32[]{:S(2)}) copy-start(f32[12,96]{1,0:T(8,128)S(1)} %get-tuple-element.37) | copy-start | bytes 13828
  208.3 49.3 %copy-start.1 = (f32[768,96]{0,1:T(8,128)S(1)}, f32[768,96]{0,1:T(8,128)}, u32[]{:S(2)}) copy-start(f32[768,96]{0,1:T(8,128)} %param.13) | copy-start | bytes 884740
  257.6 123.5 %all-gather.25.cloned.1.call-start = ((), (), s32[]{:S(2)}) async-start(), calls=%async_computation.6 | async-start | bytes 1327104 | tf_op jit(solution)/shard_map/all_gather | solution.py:56
  258.3 168.8 %all-gather.15.cloned.1.call-start = ((), (), s32[]{:S(2)}) async-start(), calls=%async_computation.1 | async-start | bytes 2654208 | tf_op jit(solution)/shard_map/all_gather | solution.py:55
  308.2 161.6 %all-gather.19.cloned.1.call-start = ((), (), s32[]{:S(2)}) async-start(), calls=%async_computation.3 | async-start | bytes 1327104 | tf_op jit(solution)/shard_map/all_gather | solution.py:29
  347.5 54.0 %copy-start.11 = (f32[96,768]{1,0:T(8,128)}, f32[96,768]{1,0:T(8,128)S(1)}, u32[]{:S(2)}) copy-start(f32[96,768]{1,0:T(8,128)S(1)} %fusion.2) | copy-start | bytes 884740
  401.5 111.4 %all-gather.27.cloned.1.call-start = ((), (), s32[]{:S(2)}) async-start(), calls=%async_computation.7 | async-start | bytes 1327104 | tf_op jit(solution)/shard_map/all_gather | solution.py:29
  403.0 151.2 %reduce-scatter.5.cloned.1.call-start = ((), (), s32[]{:S(2)}) async-start(), calls=%async_computation.11 | async-start | bytes 442368
  431.4 81.5 %copy-start.5 = (bf16[96,768]{1,0:T(8,128)(2,1)S(1)}, bf16[96,768]{1,0:T(8,128)(2,1)}, u32[]{:S(2)}) copy-start(bf16[96,768]{1,0:T(8,128)(2,1)} %multiply_convert_fusion) | copy-start | bytes 442372
  432.4 164.8 %all-gather.21.cloned.1.call-start = ((), (), s32[]{:S(2)}) async-start(), calls=%async_computation.4 | async-start | bytes 1327104 | tf_op jit(solution)/shard_map/all_gather | solution.py:29
  472.3 125.0 %copy-start.2 = (bf16[768,768]{1,0:T(8,128)(2,1)S(1)}, bf16[768,768]{1,0:T(8,128)(2,1)}, u32[]{:S(2)}) copy-start(bf16[768,768]{1,0:T(8,128)(2,1)} %all-gather.19.cloned.1.call-done) | copy-start | bytes 3538948
  472.3 125.0 %copy-start.8 = (bf16[96,768]{1,0:T(8,128)(2,1)S(1)}, bf16[96,768]{1,0:T(8,128)(2,1)}, u32[]{:S(2)}) copy-start(bf16[96,768]{1,0:T(8,128)(2,1)} %convolution_convert_fusion.3) | copy-start | bytes 442372
  472.3 167.1 %all-gather.29.cloned.1.call-start = ((), (), s32[]{:S(2)}) async-start(), calls=%async_computation.8 | async-start | bytes 1327104 | tf_op jit(solution)/shard_map/all_gather | solution.py:29
  515.4 314.3 %all-reduce.8.cloned.1.call-start = ((), (), s32[]{:S(2)}) async-start(), calls=%async_computation.13 | async-start | bytes 589824
  556.1 83.4 %copy-start.3 = (bf16[768,768]{1,0:T(8,128)(2,1)S(1)}, bf16[768,768]{1,0:T(8,128)(2,1)}, u32[]{:S(2)}) copy-start(bf16[768,768]{1,0:T(8,128)(2,1)} %all-gather.27.cloned.1.call-done) | copy-start | bytes 3538948
  556.1 83.4 %copy-start.7 = (bf16[96,768]{1,0:T(8,128)(2,1)S(1)}, bf16[96,768]{1,0:T(8,128)(2,1)}, u32[]{:S(2)}) copy-start(bf16[96,768]{1,0:T(8,128)(2,1)} %convolution_convert_fusion.1) | copy-start | bytes 442372
  556.1 317.7 %all-gather.23.cloned.1.call-start = ((), (), s32[]{:S(2)}) async-start(), calls=%async_computation.5 | async-start | bytes 1327104 | tf_op jit(solution)/shard_map/all_gather | solution.py:29
  599.8 42.2 %copy-start.20 = (f32[12,96]{1,0:T(8,128)S(1)}, f32[12,96]{1,0:T(8,128)}, u32[]{:S(2)}) copy-start(f32[12,96]{1,0:T(8,128)} %param.9) | copy-start | bytes 13828
  599.8 315.1 %all-gather.31.cloned.1.call-start = ((), (), s32[]{:S(2)}) async-start(), calls=%async_computation.9 | async-start | bytes 1327104 | tf_op jit(solution)/shard_map/all_gather | solution.py:29
  642.0 231.8 %copy-start.6 = (bf16[96,768]{1,0:T(8,128)(2,1)S(1)}, bf16[96,768]{1,0:T(8,128)(2,1)}, u32[]{:S(2)}) copy-start(bf16[96,768]{1,0:T(8,128)(2,1)} %fusion.9) | copy-start | bytes 442372
  (11 other events, 199.3 us)
Sparse Core Ops, SparseCore 0:
  11.5 196.1 all-reduce.5
  212.1 80.6 all-gather.32
  295.7 42.4 all-gather.16
  340.9 40.1 all-gather.24
  383.8 43.2 all-gather.14
  429.8 39.9 all-gather.18
  472.7 40.2 all-gather.26
  516.0 38.1 reduce-scatter.4
  556.8 40.4 all-gather.20
  599.2 40.2 all-gather.28
  643.5 186.1 all-reduce.7
  832.4 39.9 all-gather.22
  874.7 40.2 all-gather.30
where the time goes:
time: 925 us
  waiting for transfers between devices  700 us (76%)
  blocking collectives  155 us (17%)
  matrix products  37.2 us (4%)
  between operations  16.2 us (2%)
  local copies, waits for them, and re-layouts  10.1 us (1%)
    unnamed x16, waiting for transfers between devices  422 us
    all_gather x6, waiting for transfers between devices, all_rows(): lax.all_gather(for_sending(pair), 'mp', axis=0, tiled=True)  197 us
    all_gather x1, blocking collectives, per_device(): lax.all_gather(new_moment, 'dp', axis=0, tiled=True)  48.9 us
    all_gather x1, blocking collectives, per_device(): lax.all_gather(grad_piece, 'dp', axis=0, tiled=True)  48.3 us
    all_gather x1, blocking collectives, per_device(): lax.all_gather(new_master.astype(jnp.bfloat16), 'dp', axis=0, tiled=True)  41.5 us
    all_gather x1, waiting for transfers between devices, per_device(): lax.all_gather(right_basis, 'mp', axis=1, tiled=True)  33.6 us
    all_gather x1, waiting for transfers between devices, per_device(): lax.all_gather(grad_cols, 'mp', axis=1, tiled=True)  26.6 us
    all_gather x1, waiting for transfers between devices, per_device(): lax.all_gather(moment_cols, 'mp', axis=1, tiled=True)  20.7 us
  transfers between devices with their start and end apart: 13, of which 11 were waited for; matrix products, arithmetic and copies ran while one was open for 5% of the time, Pallas kernels for 0%

commit v1 on v0

--- a/solution.py
+++ b/solution.py
@@ -13,6 +13,13 @@
 quint_b = -1.25
 quint_c = 0.375
 highest = lax.Precision.HIGHEST
+
+
+def gather_over(block, axis, d):
+    size = lax.axis_size(axis)
+    tiles = jnp.stack([block for _ in range(size)])
+    tiles = lax.all_to_all(tiles, axis, split_axis=0, concat_axis=0)
+    return jnp.concatenate(tiles, axis=d)
 
 
 def for_sending(x):
@@ -51,7 +58,7 @@
         lax.all_gather(left_basis, "dp", axis=1, tiled=True),
     )
     grad_full, moment_full, right_full = (
-        lax.all_gather(grad_cols, "mp", axis=1, tiled=True),
+        gather_over(grad_cols, "mp", 1),
         lax.all_gather(moment_cols, "mp", axis=1, tiled=True),
         lax.all_gather(right_basis, "mp", axis=1, tiled=True),
     )

time: 925 us -> 883 us (0.955)
  waiting for transfers between devices: 700 us -> 652 us
    all_gather x1 -> x0, waiting for transfers between devices: 26.6 us -> none  [per_device(): lax.all_gather(grad_cols, 'mp', axis=1, tiled=True)]
    all_gather x1, waiting for transfers between devices: 33.6 us -> 9.87 us  [per_device(): lax.all_gather(right_basis, 'mp', axis=1, tiled=True)]
    unnamed x16 -> x15, waiting for transfers between devices: 422 us -> 421 us
where the time goes in v1:
time: 883 us; the launch traced here: 882 us
  waiting for transfers between devices  652 us (74%)
  blocking collectives  155 us (18%)
  matrix products  33.8 us (4%)
  between operations  16.5 us (2%)
  local copies, waits for them, and re-layouts  12.8 us (1%)
    unnamed x15, waiting for transfers between devices  421 us
    all_gather x6, waiting for transfers between devices, all_rows(): lax.all_gather(for_sending(pair), 'mp', axis=0, tiled=True)  197 us
    all_gather x1, blocking collectives, per_device(): lax.all_gather(new_moment, 'dp', axis=0, tiled=True)  48.9 us
    all_gather x1, blocking collectives, per_device(): lax.all_gather(grad_piece, 'dp', axis=0, tiled=True)  48.1 us
    all_gather x1, blocking collectives, per_device(): lax.all_gather(new_master.astype(jnp.bfloat16), 'dp', axis=0, tiled=True)  41.5 us
    all_gather x1, waiting for transfers between devices, per_device(): lax.all_gather(moment_cols, 'mp', axis=1, tiled=True)  19.2 us
  transfers between devices with their start and end apart: 13, of which 11 were waited for; matrix products, arithmetic and copies ran while one was open for 5% of the time, Pallas kernels for 0%

profile of v1, /device:TPU:2, one launch (start us, length us, event | category | flops | bytes accessed | tf_op | source)
XLA Modules:
  0.0 882.3 jit_solution(2512761754179447597)
XLA Ops:
  12.7 194.9 %all-reduce.6.cloned.1.call-done = f32[768,96]{1,0:T(8,128)} async-done(((f32[768,96]{1,0:T(8,128)}), f32[768,96]{1,0:T(8,128)}) %all-reduce.6.cloned.1.call-update) | async-done | bytes 294928
  208.4 48.1 %all-gather.1 = f32[64,12,96]{2,1,0:T(8,128)S(1)} all-gather(f32[1,12,96]{2,1,0:T(8,128)S(1)} %get-tuple-element.36), channel_id=1, replica_groups=mesh['dp'=64,'mp'=8] {'dp'}, dimensions={0}, use_global_device_ids=true | all-gather | bytes 299520 | tf_op jit(solution)/shard_map/all_gather | solution.py:56
  258.3 6.7 all-to-all-start
  265.1 48.9 %all-gather = f32[64,12,96]{2,1,0:T(8,128)S(1)} all-gather(f32[1,12,96]{2,1,0:T(8,128)S(1)} %bitcast.55), channel_id=1, replica_groups=mesh['dp'=64,'mp'=8] {'dp'}, dimensions={0}, use_global_device_ids=true | all-gather | bytes 299520 | tf_op jit(solution)/shard_map/all_gather | solution.py:57
  316.8 3.2 reshape.35
  320.0 4.1 all-to-all-done
  330.0 9.9 %all-gather.22.cloned.1.call-done = bf16[768,768]{0,1:T(8,128)(2,1)} async-done(((bf16[768,96]{0,1:T(8,128)(2,1)}), bf16[768,768]{0,1:T(8,128)(2,1)}) %all-gather.22.cloned.1.call-update) | async-done | bytes 1179664 | tf_op jit(solution)/shard_map/all_gather | solution.py:63
  342.3 16.4 %all-reduce.2 = (f32[]{:T(128)}, f32[]{:T(128)}) all-reduce(f32[]{:T(128)} %get-tuple-element.38, f32[]{:T(128)} %get-tuple-element.40), channel_id=1, replica_groups=mesh['dp'=64,'mp'=8] {'mp'}, use_global_device_ids=true, to_apply=%region_5.0 | all-reduce | flops 2 | bytes 16 | tf_op jit(solution)/shard_map/psum | solution.py:111
  361.8 2.8 fusion.35
  365.0 19.2 %all-gather.14.cloned.1.call-done = f32[768,768]{0,1:T(8,128)} async-done(((f32[768,96]{0,1:T(8,128)}), f32[768,768]{0,1:T(8,128)}) %all-gather.14.cloned.1.call-update) | async-done | bytes 2359312 | tf_op jit(solution)/shard_map/all_gather | solution.py:62
  384.2 3.7 fusion.34
  389.5 37.8 %all-gather.16.cloned.1.call-done = bf16[768,768]{1,0:T(8,128)(2,1)} async-done(((bf16[96,768]{1,0:T(8,128)(2,1)}), bf16[768,768]{1,0:T(8,128)(2,1)}) %all-gather.16.cloned.1.call-update) | async-done | bytes 1179664 | tf_op jit(solution)/shard_map/all_gather | solution.py:36
  429.9 40.4 %all-gather.24.cloned.1.call-done = bf16[768,768]{1,0:T(8,128)(2,1)} async-done(((bf16[96,768]{1,0:T(8,128)(2,1)}), bf16[768,768]{1,0:T(8,128)(2,1)}) %all-gather.24.cloned.1.call-update) | async-done | bytes 1179664 | tf_op jit(solution)/shard_map/all_gather | solution.py:36
  470.3 2.4 convolution_convert_fusion.1
  472.8 38.7 %reduce-scatter.5.cloned.1.call-done = f32[96,12]{1,0:T(8,128)} async-done(((f32[768,12]{1,0:T(8,128)}), f32[96,12]{1,0:T(8,128)}) %reduce-scatter.5.cloned.1.call-update) | async-done | bytes 4624
  513.5 41.1 %all-gather.18.cloned.1.call-done = bf16[768,768]{1,0:T(8,128)(2,1)} async-done(((bf16[96,768]{1,0:T(8,128)(2,1)}), bf16[768,768]{1,0:T(8,128)(2,1)}) %all-gather.18.cloned.1.call-update) | async-done | bytes 1179664 | tf_op jit(solution)/shard_map/all_gather | solution.py:36
  554.6 2.5 fusion.9
  557.3 39.7 %all-gather.26.cloned.1.call-done = bf16[768,768]{1,0:T(8,128)(2,1)} async-done(((bf16[96,768]{1,0:T(8,128)(2,1)}), bf16[768,768]{1,0:T(8,128)(2,1)}) %all-gather.26.cloned.1.call-update) | async-done | bytes 1179664 | tf_op jit(solution)/shard_map/all_gather | solution.py:36
  597.0 2.5 fusion.11
  599.7 187.4 %all-reduce.8.cloned.1.call-done = f32[768,96]{0,1:T(8,128)} async-done(((f32[768,96]{0,1:T(8,128)}), f32[768,96]{0,1:T(8,128)}) %all-reduce.8.cloned.1.call-update) | async-done | bytes 294928
  788.1 41.5 %all-gather.2 = bf16[64,12,96]{2,1,0:T(8,128)(2,1)S(1)} all-gather(bf16[1,12,96]{2,1,0:T(8,128)(2,1)S(1)} %copy.27), channel_id=1, replica_groups=mesh['dp'=64,'mp'=8] {'dp'}, dimensions={0}, use_global_device_ids=true | all-gather | bytes 149760 | tf_op jit(solution)/shard_map/all_gather | solution.py:89
  831.1 3.1 fusion.6
  834.2 38.1 %all-gather.28.cloned.1.call-done = bf16[768,768]{1,0:T(8,128)(2,1)} async-done(((bf16[96,768]{1,0:T(8,128)(2,1)}), bf16[768,768]{1,0:T(8,128)(2,1)}) %all-gather.28.cloned.1.call-update) | async-done | bytes 1179664 | tf_op jit(solution)/shard_map/all_gather | solution.py:36
  872.3 3.2 fusion.4
  (99 shorter events, 29.4 us)
Async XLA Ops:
  7.2 200.5 %copy-start.21 = (f32[12,96]{1,0:T(8,128)S(1)}, f32[12,96]{1,0:T(8,128)}, u32[]{:S(2)}) copy-start(f32[12,96]{1,0:T(8,128)} %param.10) | copy-start | bytes 13828
  7.2 200.4 %all-reduce.6.cloned.1.call-start = ((), (), s32[]{:S(2)}) async-start(), calls=%async_computation.12 | async-start | bytes 786432
  9.3 307.5 %all-gather.30.cloned.1.call-start = ((), (), s32[]{:S(2)}) async-start(), calls=%async_computation.10 | async-start | bytes 1597440 | tf_op jit(solution)/shard_map/all_gather | solution.py:58
  10.0 329.8 %all-gather.22.cloned.1.call-start = ((), (), s32[]{:S(2)}) async-start(), calls=%async_computation.6 | async-start | bytes 1327104 | tf_op jit(solution)/shard_map/all_gather | solution.py:63
  208.4 56.7 %copy-start.17 = (f32[12,96]{1,0:T(8,128)}, f32[12,96]{1,0:T(8,128)S(1)}, u32[]{:S(2)}) copy-start(f32[12,96]{1,0:T(8,128)S(1)} %get-tuple-element.37) | copy-start | bytes 13828
  258.3 65.8 %all-to-all-start = ((f32[8,768,96]{1,2,0:T(8,128)}), f32[8,768,96]{1,2,0:T(8,128)S(1)}, u32[]{:S(2)}, u32[]{:S(2)}) async-start(f32[8,768,96]{1,2,0:T(8,128)} %stack.2), calls=%async_computation | async-start | bytes 4718592 | tf_op jit(solution)/shard_map/all_to_all | solution.py:21
  265.0 119.1 %all-gather.14.cloned.1.call-start = ((), (), s32[]{:S(2)}) async-start(), calls=%async_computation.2 | async-start | bytes 2654208 | tf_op jit(solution)/shard_map/all_gather | solution.py:62
  316.7 110.7 %all-gather.16.cloned.1.call-start = ((), (), s32[]{:S(2)}) async-start(), calls=%async_computation.3 | async-start | bytes 1327104 | tf_op jit(solution)/shard_map/all_gather | solution.py:36
  360.1 110.2 %all-gather.24.cloned.1.call-start = ((), (), s32[]{:S(2)}) async-start(), calls=%async_computation.7 | async-start | bytes 1327104 | tf_op jit(solution)/shard_map/all_gather | solution.py:36
  361.5 150.0 %reduce-scatter.5.cloned.1.call-start = ((), (), s32[]{:S(2)}) async-start(), calls=%async_computation.11 | async-start | bytes 442368
  387.9 39.5 %copy-start.4 = (bf16[96,768]{1,0:T(8,128)(2,1)S(1)}, bf16[96,768]{1,0:T(8,128)(2,1)}, u32[]{:S(2)}) copy-start(bf16[96,768]{1,0:T(8,128)(2,1)} %multiply_convert_fusion.1) | copy-start | bytes 442372
  388.5 81.8 %copy-start.5 = (bf16[96,768]{1,0:T(8,128)(2,1)S(1)}, bf16[96,768]{1,0:T(8,128)(2,1)}, u32[]{:S(2)}) copy-start(bf16[96,768]{1,0:T(8,128)(2,1)} %multiply_convert_fusion) | copy-start | bytes 442372
  389.5 165.1 %all-gather.18.cloned.1.call-start = ((), (), s32[]{:S(2)}) async-start(), calls=%async_computation.4 | async-start | bytes 1327104 | tf_op jit(solution)/shard_map/all_gather | solution.py:36
  429.8 124.8 %copy-start.1 = (bf16[768,768]{1,0:T(8,128)(2,1)S(1)}, bf16[768,768]{1,0:T(8,128)(2,1)}, u32[]{:S(2)}) copy-start(bf16[768,768]{1,0:T(8,128)(2,1)} %all-gather.16.cloned.1.call-done) | copy-start | bytes 3538948
  429.8 124.8 %copy-start.8 = (bf16[96,768]{1,0:T(8,128)(2,1)S(1)}, bf16[96,768]{1,0:T(8,128)(2,1)}, u32[]{:S(2)}) copy-start(bf16[96,768]{1,0:T(8,128)(2,1)} %convolution_convert_fusion.3) | copy-start | bytes 442372
  429.8 167.1 %all-gather.26.cloned.1.call-start = ((), (), s32[]{:S(2)}) async-start(), calls=%async_computation.8 | async-start | bytes 1327104 | tf_op jit(solution)/shard_map/all_gather | solution.py:36
  472.8 314.2 %all-reduce.8.cloned.1.call-start = ((), (), s32[]{:S(2)}) async-start(), calls=%async_computation.13 | async-start | bytes 589824
  513.4 83.5 %copy-start.2 = (bf16[768,768]{1,0:T(8,128)(2,1)S(1)}, bf16[768,768]{1,0:T(8,128)(2,1)}, u32[]{:S(2)}) copy-start(bf16[768,768]{1,0:T(8,128)(2,1)} %all-gather.24.cloned.1.call-done) | copy-start | bytes 3538948
  513.5 83.5 %copy-start.7 = (bf16[96,768]{1,0:T(8,128)(2,1)S(1)}, bf16[96,768]{1,0:T(8,128)(2,1)}, u32[]{:S(2)}) copy-start(bf16[96,768]{1,0:T(8,128)(2,1)} %convolution_convert_fusion.1) | copy-start | bytes 442372
  513.5 317.6 %all-gather.20.cloned.1.call-start = ((), (), s32[]{:S(2)}) async-start(), calls=%async_computation.5 | async-start | bytes 1327104 | tf_op jit(solution)/shard_map/all_gather | solution.py:36
  557.2 42.3 %copy-start.20 = (f32[12,96]{1,0:T(8,128)S(1)}, f32[12,96]{1,0:T(8,128)}, u32[]{:S(2)}) copy-start(f32[12,96]{1,0:T(8,128)} %param.9) | copy-start | bytes 13828
  557.2 315.1 %all-gather.28.cloned.1.call-start = ((), (), s32[]{:S(2)}) async-start(), calls=%async_computation.9 | async-start | bytes 1327104 | tf_op jit(solution)/shard_map/all_gather | solution.py:36
  599.5 231.6 %copy-start.6 = (bf16[96,768]{1,0:T(8,128)(2,1)S(1)}, bf16[96,768]{1,0:T(8,128)(2,1)}, u32[]{:S(2)}) copy-start(bf16[96,768]{1,0:T(8,128)(2,1)} %fusion.9) | copy-start | bytes 442372
  831.1 41.2 %copy-start.9 = (bf16[96,768]{1,0:T(8,128)(2,1)S(1)}, bf16[96,768]{1,0:T(8,128)(2,1)}, u32[]{:S(2)}) copy-start(bf16[96,768]{1,0:T(8,128)(2,1)} %fusion.11) | copy-start | bytes 442372
  (11 other events, 118.4 us)
Sparse Core Ops, SparseCore 0:
  11.5 196.1 all-reduce.5
  212.1 80.6 all-gather.29
  295.6 44.1 all-gather.21
  342.5 41.5 all-gather.13
  386.9 40.4 all-gather.15
  430.1 40.2 all-gather.23
  473.3 38.1 reduce-scatter.4
  514.2 40.4 all-gather.17
  556.7 40.2 all-gather.25
  600.9 186.1 all-reduce.7
  789.9 39.8 all-gather.19
  832.0 40.2 all-gather.27
